TPU v7x, 32 devices: a whole 2x2x4 slice. The times are simulated.
32 devices in a mesh: groups: 2 (over y), seq: 4 (over x, core), fsdp: 4 (over z).
Axes of the slice: x: 2, y: 2, z: 4, core: 2. Of those that a mesh axis runs over, the one named last changes fastest.
Arguments:
- tokens: bfloat16 [16, 512, 1536], P(('groups', 'fsdp'), 'seq'), parts along dimension 0, may hold values from -6 to 6
- in_weight: bfloat16 [1536, 4608], P(None, 'fsdp'), may hold values from -0.15625 to 0.15625
- short_weight: float32 [3, 4608], replicated, may hold values from -3.5 to 3.5
- basis_in: float32 [17, 64], replicated, may hold values from -4 to 4
- basis_bias: float32 [64], replicated, may hold values from -3.140625 to 3.140625
- basis_mid: float32 [64, 64], replicated, may hold values from -1.5 to 1.5
- basis_shift: float32 [64], replicated, may hold values from -3.140625 to 3.140625
- response_out: float32 [2, 64, 1536], P(None, None, 'fsdp'), may hold values from -0.0234375 to 0.0234375
- skip_gain: float32 [1536], P('fsdp'), may hold values from -4 to 4
- block_counts: int32 [16, 4], P(('groups', 'fsdp'), 'seq'), parts along dimension 0, may hold values from 1 to 128, as said below
Outputs:
- mixed: bfloat16 [16, 512, 1536], P(('groups', 'fsdp'), 'seq'), parts along dimension 0
There are 2 independent parts, one for each index of `groups`. A program takes and returns all parts, laid end to end along the dimension named above; an argument that names none is the same for every part. Nothing has to cross between parts.
Inputs may be any that keep to these rules, and one draw needn't show every extreme that they name: `block_counts`: in every table one block holds all 128 tokens and another holds a single token.
All inputs are finite; a program needn't handle non-finite values.
Results may differ from a plain program's by a relative error of at most 0.007.
Values may be sent and summed in bfloat16 or wider, within the bound.
No kernel may reach another device: no remote copies, remote signals or barrier semaphores. Data moves between devices by JAX's collectives and lax.ppermute only.
A program may use at most 128 MiB of HBM per device.

v0:
```python
import jax
import jax.numpy as jnp
from jax import lax
from jax.sharding import PartitionSpec as P


def padded_2(cells, sides, width):
    for axis, dim in sides:
        count = lax.axis_size(axis)
        ends = count - 1
        head = lax.slice_in_dim(cells, 0, width, axis=dim)
        tail = lax.slice_in_dim(cells, cells.shape[dim] - width, cells.shape[dim], axis=dim)
        cells = jnp.concatenate(
            [
                lax.ppermute(tail, axis, [(i, (i + 1) % count) for i in range(ends)]),
                cells,
                lax.ppermute(head, axis, [((i + 1) % count, i) for i in range(ends)]),
            ],
            axis=dim,
        )
    return cells


def filter_basis(lag_values, total_len, basis_in, basis_bias, basis_mid, basis_shift):
    band_count = (basis_in.shape[0] - 1) // 2
    distance = jnp.abs(lag_values)
    periods = (2 ** (jnp.arange(band_count, dtype=jnp.int32) + 2) + 1).astype(jnp.int32)
    angles = (
        2.0
        * jnp.pi
        * (distance[:, None] % periods[None, :]).astype(jnp.float32)
        / periods[None, :].astype(jnp.float32)
    )
    linear = distance.astype(jnp.float32)[:, None] / total_len
    encoded = jnp.concatenate([linear, jnp.cos(angles), jnp.sin(angles)], axis=1)
    hidden = jnp.sin(jnp.dot(encoded, basis_in, precision=lax.Precision.HIGHEST) + basis_bias)
    return jnp.sin(jnp.dot(hidden, basis_mid, precision=lax.Precision.HIGHEST) + basis_shift)


def forward_table(block_len):
    period = 2 * block_len
    frequency = jnp.arange(block_len, dtype=jnp.int32)[:, None]
    samples = jnp.arange(period, dtype=jnp.int32)[None, :]
    phases = 2.0 * jnp.pi / period * (frequency * samples % period).astype(jnp.float32)
    alternate = (1 - 2 * (samples % 2)).astype(jnp.float32)
    real_rows = jnp.cos(phases)
    imag_rows = jnp.where(frequency == 0, alternate, -jnp.sin(phases))
    return jnp.concatenate([real_rows, imag_rows], axis=0)


def inverse_table(block_len):
    period = 2 * block_len
    places = jnp.arange(block_len, dtype=jnp.int32)[:, None]
    frequency = jnp.arange(block_len, dtype=jnp.int32)[None, :]
    phases = 2.0 * jnp.pi / period * (places * frequency % period).astype(jnp.float32)
    alternate = (1 - 2 * (places % 2)).astype(jnp.float32)
    real_cols = jnp.where(frequency == 0, 1.0, 2.0 * jnp.cos(phases)) / period
    imag_cols = jnp.where(frequency == 0, alternate, -2.0 * jnp.sin(phases)) / period
    return jnp.concatenate([real_cols, imag_cols], axis=1)


def packed_product(response, signal, block_len):
    first_slot = (jnp.arange(block_len) == 0)[:, None]
    resp_real = response[..., :block_len, :]
    resp_imag = response[..., block_len:, :]
    sig_real = signal[..., :block_len, :]
    sig_imag = signal[..., block_len:, :]
    cross_term = resp_imag * sig_imag
    prod_real = resp_real * sig_real - jnp.where(first_slot, 0.0, cross_term)
    prod_imag = jnp.where(first_slot, cross_term, resp_real * sig_imag + resp_imag * sig_real)
    return jnp.concatenate([prod_real, prod_imag], axis=-2)


def shards(
    tokens,
    in_weight,
    short_weight,
    basis_in,
    basis_bias,
    basis_mid,
    basis_shift,
    response_out,
    skip_gain,
    block_counts,
):
    seq_dev, block_len, width = tokens.shape
    group_tokens = lax.all_gather(tokens, "fsdp", axis=0, tiled=True)
    group_rows = group_tokens.shape[0]
    local_cols = in_weight.shape[1]
    partial = jnp.dot(
        group_tokens.reshape(group_rows * block_len, width),
        in_weight,
        preferred_element_type=jnp.float32,
    ).astype(jnp.bfloat16)
    partial = partial.reshape(group_rows, block_len, local_cols)
    projected = lax.all_to_all(partial, "fsdp", 0, 2, tiled=True)
    padded = padded_2(projected, (("seq", 1),), 1)
    shorted = (
        short_weight[0] * padded[:, :-2]
        + short_weight[1] * padded[:, 1:-1]
        + short_weight[2] * padded[:, 2:]
    )
    query_gate = shorted[:, :, :width]
    key_part = shorted[:, :, width : 2 * width]
    value_part = shorted[:, :, 2 * width :]
    valid_mask = (jnp.arange(block_len, dtype=jnp.int32)[None, :] < block_counts).astype(
        jnp.float32
    )
    carried = (key_part * value_part * valid_mask[:, :, None]).astype(jnp.bfloat16)
    local_ch = skip_gain.shape[0]
    params = jnp.concatenate(
        [response_out.reshape(2 * response_out.shape[1], local_ch), skip_gain[None, :]], axis=0
    )
    gathered = lax.all_gather(params, "fsdp", axis=0, tiled=False)
    gathered = jnp.transpose(gathered, (1, 0, 2)).reshape(params.shape[0], width)
    stacked_out = gathered[:-1]
    full_skip = gathered[-1]
    seq_count = lax.axis_size("seq")
    position = lax.axis_index("seq")
    total_len = float(seq_count * block_len)
    forward = forward_table(block_len)
    forward_half = forward[:, :block_len]
    half_hi = forward_half.astype(jnp.bfloat16)
    half_lo = (forward_half - half_hi.astype(jnp.float32)).astype(jnp.bfloat16)
    inverse = inverse_table(block_len)
    circular = jnp.arange(2 * block_len, dtype=jnp.int32)
    wrapped = jnp.where(circular < block_len, circular, circular - 2 * block_len)
    piece = lax.all_gather(carried, "seq", axis=1, tiled=True)
    block_total = piece.shape[1] // block_len
    chunk = min(block_total, 4)

    def chunk_spectrum(first, rows):
        offsets = (position - first - jnp.arange(chunk, dtype=jnp.int32)) * block_len
        lag_values = (offsets[:, None] + wrapped[None, :]).reshape(-1)
        basis_rows = filter_basis(
            lag_values, total_len, basis_in, basis_bias, basis_mid, basis_shift
        )
        ahead_mask = (lag_values >= 0).astype(jnp.float32)[:, None]
        paired = jnp.concatenate([basis_rows * ahead_mask, basis_rows * (1.0 - ahead_mask)], axis=1)
        paired = paired.reshape(chunk, 2 * block_len, paired.shape[-1])
        paired_spec = jnp.einsum("gf,bfk->bgk", forward, paired, precision=lax.Precision.HIGHEST)
        response = jnp.einsum("bgk,kd->bgd", paired_spec, stacked_out, precision=lax.Precision.HIGH)
        blocks = rows.reshape(seq_dev, chunk, block_len, width)
        signal = jnp.einsum(
            "fc,sbcd->sbfd", half_hi, blocks, preferred_element_type=jnp.float32
        ) + jnp.einsum("fc,sbcd->sbfd", half_lo, blocks, preferred_element_type=jnp.float32)
        total = packed_product(response[None, 0], signal[:, 0], block_len)
        for index in range(1, chunk):
            total = total + packed_product(response[None, index], signal[:, index], block_len)
        return total

    if chunk == block_total:
        spectrum = chunk_spectrum(0, piece)
    else:

        def one_chunk(chunk_index, carry):
            rows = lax.dynamic_slice_in_dim(
                piece, chunk_index * chunk * block_len, chunk * block_len, 1
            )
            return carry + chunk_spectrum(chunk_index * chunk, rows)

        spectrum = lax.fori_loop(
            0,
            block_total // chunk,
            one_chunk,
            jnp.zeros((seq_dev, 2 * block_len, width), jnp.float32),
        )
    conv = jnp.einsum("if,sfd->sid", inverse, spectrum, precision=lax.Precision.HIGH)
    return (query_gate * (conv + full_skip * carried.astype(jnp.float32))).astype(jnp.bfloat16)


def solution(mesh):
    placed = (
        P(("groups", "fsdp"), "seq", None),
        P(None, "fsdp"),
        P(),
        P(),
        P(),
        P(),
        P(),
        P(None, None, "fsdp"),
        P("fsdp"),
        P(("groups", "fsdp"), "seq"),
    )
    return jax.shard_map(
        shards,
        mesh=mesh,
        in_specs=placed,
        out_specs=P(("groups", "fsdp"), "seq", None),
        check_vma=False,
    )
```

profile of v0, /device:TPU:0, one launch (start us, length us, event | category | flops | bytes accessed | tf_op | source)
XLA Modules:
  0.0 243.3 jit_solution(17354887653073094636)
XLA Ops:
  6.5 0.0 all-gather.5.cloned.1.call-start
  6.5 0.7 all-gather.5.cloned.1.call-update
  7.3 67.9 %all-gather.5.cloned.1.call-done = bf16[8,128,1536]{2,1,0:T(8,128)(2,1)} async-done(((bf16[2,128,1536]{2,1,0:T(8,128)(2,1)}), bf16[8,128,1536]{2,1,0:T(8,128)(2,1)}) %all-gather.5.cloned.1.call-update) | async-done | bytes 3145744 | tf_op jit(solution)/shard_map/all_gather | solution.py:87
  75.2 0.0 copy-done
  75.2 7.5 %convolution_convert_fusion = bf16[1024,1152]{1,0:T(8,128)(2,1)} fusion(bf16[1024,1536]{1,0:T(8,128)(2,1)} %bitcast.106, bf16[1536,1152]{1,0:T(8,128)(2,1)S(1)} %copy-done), kind=kOutput, calls=%fused_computation.2 | convolution fusion | flops 3625058304 | bytes 9043968 | tf_op jit(solution)/shard_map/dot_general | solution.py:90
  82.7 3.8 %all-to-all-start = ((bf16[8,128,1152]{2,1,0:T(8,128)(2,1)}), bf16[8,128,1152]{2,1,0:T(8,128)(2,1)S(1)}, u32[]{:S(2)}, u32[]{:S(2)}) async-start(bf16[8,128,1152]{2,1,0:T(8,128)(2,1)} %bitcast.99), calls=%async_computation | async-start | bytes 4718592 | tf_op jit(solution)/shard_map/all_to_all | solution.py:96
  86.5 0.0 all-gather.7.cloned.1.call-start
  86.5 0.1 slice_reduce_fusion.2
  86.7 0.1 compare_convert_fusion
  86.8 53.7 %all-to-all-done = bf16[8,128,1152]{2,1,0:T(8,128)(2,1)S(1)} async-done(((bf16[8,128,1152]{2,1,0:T(8,128)(2,1)}), bf16[8,128,1152]{2,1,0:T(8,128)(2,1)S(1)}, u32[]{:S(2)}, u32[]{:S(2)}) %all-to-all-start) | async-done | bytes 2359328 | tf_op jit(solution)/shard_map/all_to_all | solution.py:96
  140.5 1.4 copy-done.4
  141.9 3.0 %copy.19 = bf16[4,2,128,1152]{2,3,0,1:T(8,128)(2,1)S(1)} copy(bf16[4,2,128,1152]{3,2,1,0:T(8,128)(2,1)} %bitcast.96) | data formatting | bytes 4718592 | tf_op jit(solution)/shard_map/all_to_all | solution.py:96
  145.0 2.9 %fusion.85 = (bf16[2,1,4608]{1,2,0:T(8,128)(2,1)}, bf16[2,1,4608]{1,2,0:T(8,128)(2,1)}) fusion(bf16[2,128,4608]{1,2,0:T(8,128)(2,1)S(1)} %bitcast.92), kind=kLoop, calls=%fused_computation.153 | loop fusion | bytes 73728 | tf_op jit(solution)/shard_map/slice | solution.py:12
  147.9 2.1 copy.22
  150.0 1.3 collective-permute-start.1
  151.3 2.1 copy.20
  153.4 3.0 %collective-permute-start = (bf16[2,1,4608]{2,0,1:T(2,128)(2,1)S(1)}, bf16[2,1,4608]{2,0,1:T(2,128)(2,1)S(1)}, u32[]{:S(2)}, u32[]{:S(2)}) collective-permute-start(bf16[2,1,4608]{2,0,1:T(2,128)(2,1)S(1)} %copy.20), channel_id=1, source_target_pairs={{0,4},{4,8},{8,12},{1,5},{5,9},{9,13},{2,6},{6,10},{10,14},{3,7},{... | collective-permute-start | bytes 55304 | tf_op jit(solution)/shard_map/ppermute | solution.py:15
  156.5 0.0 collective-permute-done.1
  156.5 2.0 copy.23
  158.5 0.0 collective-permute-done
  158.5 2.0 copy.21
  160.4 6.3 %multiply_add_fusion = f32[2,128,4608]{1,2,0:T(8,128)S(1)} fusion(bf16[2,128,4608]{1,2,0:T(8,128)(2,1)S(1)} %bitcast.93, bf16[2,1,4608]{1,2,0:T(8,128)(2,1)} %copy.23, bf16[2,1,4608]{1,2,0:T(8,128)(2,1)} %copy.21, f32[4608]{0:T(1024)S(1)} %get-tuple-element.6, f32[4608]{0:T(1024)S(1)} %get-tuple-element.7, f32[4608]{0:T(1024)S(1)} %get-tuple-element.5), kind=kLoop, calls=%fused_computation.1 | loop fusion | flops 16515072 | bytes 7170048 | tf_op jit(solution)/shard_map/add | solution.py:99
  166.7 2.1 copy-done.2
  168.8 1.0 fusion.22
  169.9 0.0 all-gather.7.cloned.1.call-update
  169.9 0.1 convert_bitcast_fusion
  170.0 0.1 fusion.68
  170.1 0.1 fusion.71
  170.2 0.0 copy-done.18
  170.2 18.9 %all-gather.1 = f32[4,129,384]{2,1,0:T(8,128)S(1)} all-gather(f32[1,129,384]{2,1,0:T(8,128)S(1)} %maximum_bitcast_fusion), channel_id=2, replica_groups=mesh['groups'=2,'seq'=4,'fsdp'=4] {'fsdp'}, dimensions={0}, use_global_device_ids=true | all-gather | bytes 990720 | tf_op jit(solution)/shard_map/all_gather | solution.py:114
  189.2 0.1 slice.154
  189.2 0.5 copy.24
  189.7 0.3 reshape.231
  190.2 0.6 fusion.65
  190.7 0.0 copy-done.17
  190.8 2.5 %fusion.26 = f32[1024,64]{1,0:T(8,128)S(1)} fusion(f32[17,64]{1,0:T(8,128)S(1)} %copy-done.17, f32[64]{0:T(128)S(1)} %copy-done.20, f32[1024,8]{0,1:T(8,128)S(1)} %get-tuple-element.33, f32[1024,8]{0,1:T(8,128)S(1)} %get-tuple-element.32, f32[1024,1]{0,1:T(1,128)S(1)} %bitcast.104), kind=kOutput, calls=%fused_computation.45 | convolution fusion | flops 13469696 | bytes 336384 | tf_op jit(solution)/shard_map/dot_general | solution.py:36
  193.3 0.0 copy-done.16
  193.3 0.0 copy-done.19
  193.3 1.5 broadcast_multiply_fusion.1
  194.9 0.9 select_multiply_fusion.1
  195.8 0.5 negate_select_fusion.2
  196.4 0.7 convolution_bitcast_fusion
  197.1 2.7 %fusion.86 = f32[4,256,1536]{2,1,0:T(8,128)S(1)} fusion(f32[4,256,128]{2,1,0:T(8,128)S(1)} %convolution_bitcast_fusion, f32[128,1536,1]{1,0,2:T(8,128)S(1)} %reshape.231), kind=kOutput, calls=%fused_computation.154 | convolution fusion | flops 1207959552 | bytes 7602176 | tf_op jit(solution)/shard_map/bgk,kd->bgd/dot_general | solution.py:142
  199.7 2.7 %slice_bitcast_fusion.5 = (f32[128,1536]{1,0:T(8,128)}, f32[128,1536]{1,0:T(8,128)}, f32[128,1536]{1,0:T(8,128)}, f32[128,1536]{1,0:T(8,128)}, f32[128,1536]{1,0...) fusion(f32[4,256,1536]{2,1,0:T(8,128)S(1)} %fusion.86), kind=kLoop, calls=%fused_computation.49 | loop fusion | bytes 12582912 | tf_op jit(solution)/shard_map/mul | solution.py:69
  202.5 3.2 %copy.25 = bf16[2,512,1536]{2,1,0:T(8,128)(2,1)S(1)} copy(bf16[2,512,1536]{1,2,0:T(8,128)(2,1)} %all-gather.7.cloned.1.call-done) | data formatting | bytes 6291456 | tf_op jit(solution)/shard_map/all_gather | solution.py:128
  205.7 1.8 fusion.51
  207.4 6.3 %add_bitcast_fusion = f32[2,4,256,1536]{3,2,1,0:T(8,128)} fusion(f32[2,4,1536,256]{2,3,1,0:T(8,128)S(1)} %fusion.51, bf16[2,4,128,1536]{3,2,1,0:T(8,128)(2,1)S(1)} %bitcast.95, f32[128,256]{1,0:T(8,128)S(1)} %get-tuple-element.41, f32[128,256]{1,0:T(8,128)S(1)} %get-tuple-element.40), kind=kOutput, calls=%fused_computation | convolution fusion | flops 808615936 | bytes 28573696 | tf_op jit(solution)/shard_map/fc,sbcd->sbfd/dot_general | solution.py:146
  213.7 8.6 %slice_bitcast_fusion = (f32[2,256,1536]{2,1,0:T(8,128)S(1)}, f32[2,256,1536]{2,1,0:T(8,128)S(1)}, f32[2,256,1536]{2,1,0:T(8,128)}, f32[2,256,1536]{2,1,0:T(8,128)}) fusion(f32[2,4,256,1536]{3,2,1,0:T(8,128)} %add_bitcast_fusion), kind=kLoop, calls=%fused_computation.3 | loop fusion | bytes 25165824 | tf_op jit(solution)/shard_map/squeeze | solution.py:149
  222.3 0.0 copy-start.8
  222.3 0.0 copy-start.9
  222.3 0.0 copy-start.10
  222.3 0.0 copy-start.11
  222.3 3.1 %select_subtract_fusion.3 = (f32[2,128,1536]{2,1,0:T(8,128)S(1)}, f32[2,128,1536]{2,1,0:T(8,128)S(1)}) fusion(f32[2,256,1536]{2,1,0:T(8,128)} %get-tuple-element.10, f32[128,1536]{1,0:T(8,128)} %get-tuple-element.18, f32[128,1536]{1,0:T(8,128)} %get-tuple-element.19, pred[128]{0:T(512)(128)(4,1)S(1)} %iota_compare_fusion), kind=kLoop, calls=%fused_computation.38 | loop fusion | flops 3145728 | bytes 7864448 | tf_op jit(solution)/shard_map/sub | solution.py:69
  225.5 0.1 copy-done.3
  225.6 0.2 copy-done.6
  225.8 0.2 copy-done.7
  226.0 0.2 copy-done.8
  226.3 0.2 copy-done.9
  226.5 0.2 copy-done.10
  226.7 0.2 copy-done.11
  226.9 1.9 select_subtract_fusion
  228.9 0.0 copy-start.1
  228.9 5.3 %fusion.23 = bf16[2,128,1536]{1,2,0:T(8,128)(2,1)} fusion(f32[2,128,4608]{1,2,0:T(8,128)} %copy-done.2, f32[2,128,1536]{2,1,0:T(8,128)S(1)} %get-tuple-element.27, f32[2,128,1536]{2,1,0:T(8,128)S(1)} %get-tuple-element.26, f32[2,128,1536]{2,1,0:T(8,128)S(1)} %get-tuple-element.36, f32[2,128,1536]{2,1,0:T(8,128)S(1)} %get-tuple-element.37, ...), kind=kOutput, calls=%fused_computation.30 | convolution fusion | flops 611483648 | bytes 15865856 | tf_op jit(solution)/shard_map/if,sfd->sid/dot_general | solution.py:168
  234.2 2.3 copy.30
  (42 shorter events, 0.2 us)
Async XLA Ops:
  6.5 68.6 %copy-start = (bf16[1536,1152]{1,0:T(8,128)(2,1)S(1)}, bf16[1536,1152]{1,0:T(8,128)(2,1)}, u32[]{:S(2)}) copy-start(bf16[1536,1152]{1,0:T(8,128)(2,1)} %param.11) | copy-start | bytes 10616836
  6.5 68.6 %all-gather.5.cloned.1.call-start = ((), (), s32[]{:S(2)}) async-start(), calls=%async_computation.1 | async-start | bytes 3932160 | tf_op jit(solution)/shard_map/all_gather | solution.py:87
  82.7 3.8 %copy-start.15 = (f32[3,4608]{1,0:T(4,128)S(1)}, f32[3,4608]{1,0:T(4,128)}, u32[]{:S(2)}) copy-start(f32[3,4608]{1,0:T(4,128)} %param.12) | copy-start | bytes 165892
  82.7 4.0 %copy-start.21 = (s32[2,1]{0,1:T(1,128)S(1)}, s32[2,1]{0,1:T(1,128)}, u32[]{:S(2)}) copy-start(s32[2,1]{0,1:T(1,128)} %param.19) | copy-start | bytes 28
  82.7 57.8 %all-to-all-start = ((bf16[8,128,1152]{2,1,0:T(8,128)(2,1)}), bf16[8,128,1152]{2,1,0:T(8,128)(2,1)S(1)}, u32[]{:S(2)}, u32[]{:S(2)}) async-start(bf16[8,128,1152]{2,1,0:T(8,128)(2,1)} %bitcast.99), calls=%async_computation | async-start | bytes 4718592 | tf_op jit(solution)/shard_map/all_to_all | solution.py:96
  86.5 116.0 %all-gather.7.cloned.1.call-start = ((), (), s32[]{:S(2)}) async-start(), calls=%async_computation.2 | async-start | bytes 3932160 | tf_op jit(solution)/shard_map/all_gather | solution.py:128
  140.5 1.4 copy-start.4
  150.0 6.5 %collective-permute-start.1 = (bf16[2,1,4608]{2,0,1:T(2,128)(2,1)S(1)}, bf16[2,1,4608]{2,0,1:T(2,128)(2,1)S(1)}, u32[]{:S(2)}, u32[]{:S(2)}) collective-permute-start(bf16[2,1,4608]{2,0,1:T(2,128)(2,1)S(1)} %copy.22), channel_id=1, source_target_pairs={{4,0},{8,4},{12,8},{5,1},{9,5},{13,9},{6,2},{10,6},{14,10},{7,3},{... | collective-permute-start | bytes 55304 | tf_op jit(solution)/shard_map/ppermute | solution.py:17
  153.4 5.0 %collective-permute-start = (bf16[2,1,4608]{2,0,1:T(2,128)(2,1)S(1)}, bf16[2,1,4608]{2,0,1:T(2,128)(2,1)S(1)}, u32[]{:S(2)}, u32[]{:S(2)}) collective-permute-start(bf16[2,1,4608]{2,0,1:T(2,128)(2,1)S(1)} %copy.20), channel_id=1, source_target_pairs={{0,4},{4,8},{8,12},{1,5},{5,9},{9,13},{2,6},{6,10},{10,14},{3,7},{... | collective-permute-start | bytes 55304 | tf_op jit(solution)/shard_map/ppermute | solution.py:15
  166.7 2.1 copy-start.2
  168.8 1.3 copy-start.18
  168.8 1.3 copy-start.14
  189.1 1.6 copy-start.17
  189.1 1.6 copy-start.20
  189.1 4.1 %copy-start.16 = (f32[64,64]{1,0:T(8,128)S(1)}, f32[64,64]{1,0:T(8,128)}, u32[]{:S(2)}) copy-start(f32[64,64]{1,0:T(8,128)} %param.15) | copy-start | bytes 49156
  189.2 4.1 %copy-start.19 = (f32[64]{0:T(128)S(1)}, f32[64]{0:T(128)}, u32[]{:S(2)}) copy-start(f32[64]{0:T(128)} %param.16) | copy-start | bytes 772
  222.3 3.3 %copy-start.3 = (f32[2,256,1536]{2,1,0:T(8,128)S(1)}, f32[2,256,1536]{2,1,0:T(8,128)}, u32[]{:S(2)}) copy-start(f32[2,256,1536]{2,1,0:T(8,128)} %get-tuple-element.11) | copy-start | bytes 9437188
  222.3 3.5 %copy-start.6 = (f32[128,1536]{1,0:T(8,128)S(1)}, f32[128,1536]{1,0:T(8,128)}, u32[]{:S(2)}) copy-start(f32[128,1536]{1,0:T(8,128)} %get-tuple-element.12) | copy-start | bytes 2359300
  222.3 3.7 %copy-start.7 = (f32[128,1536]{1,0:T(8,128)S(1)}, f32[128,1536]{1,0:T(8,128)}, u32[]{:S(2)}) copy-start(f32[128,1536]{1,0:T(8,128)} %get-tuple-element.13) | copy-start | bytes 2359300
  222.3 4.0 %copy-start.8 = (f32[128,1536]{1,0:T(8,128)S(1)}, f32[128,1536]{1,0:T(8,128)}, u32[]{:S(2)}) copy-start(f32[128,1536]{1,0:T(8,128)} %get-tuple-element.14) | copy-start | bytes 2359300
  222.3 4.2 %copy-start.9 = (f32[128,1536]{1,0:T(8,128)S(1)}, f32[128,1536]{1,0:T(8,128)}, u32[]{:S(2)}) copy-start(f32[128,1536]{1,0:T(8,128)} %get-tuple-element.15) | copy-start | bytes 2359300
  222.3 4.4 %copy-start.10 = (f32[128,1536]{1,0:T(8,128)S(1)}, f32[128,1536]{1,0:T(8,128)}, u32[]{:S(2)}) copy-start(f32[128,1536]{1,0:T(8,128)} %get-tuple-element.16) | copy-start | bytes 2359300
  222.3 4.6 %copy-start.11 = (f32[128,1536]{1,0:T(8,128)S(1)}, f32[128,1536]{1,0:T(8,128)}, u32[]{:S(2)}) copy-start(f32[128,1536]{1,0:T(8,128)} %get-tuple-element.17) | copy-start | bytes 2359300
  226.9 1.9 copy-start.5
  226.9 1.9 copy-start.12
  226.9 1.9 copy-start.13
  228.9 7.6 %copy-start.1 = (bf16[1536,1152]{1,0:T(8,128)(2,1)S(1)}, bf16[1536,1152]{1,0:T(8,128)(2,1)}, u32[]{:S(2)}) copy-start(bf16[1536,1152]{1,0:T(8,128)(2,1)} %param.11) | copy-start | bytes 10616836
Sparse Core Ops, SparseCore 0:
  8.9 66.1 all-gather.4
  170.0 28.6 all-gather.6
where the time goes:
time: 244 us; the launch traced here: 243 us
  waiting for transfers between devices  122 us (50%)
  local copies, waits for them, and re-layouts  37 us (15%)
  matrix products  28.2 us (12%)
  blocking collectives  18.9 us (8%)
  other arithmetic  14.8 us (6%)
  between operations  13.8 us (6%)
  starting transfers between devices  8.13 us (3%)
    all_gather x1, waiting for transfers between devices, shards(): group_tokens = lax.all_gather(tokens, 'fsdp', axis=0, tiled=True)  67.9 us
    all_to_all x1, waiting for transfers between devices, shards(): projected = lax.all_to_all(partial, 'fsdp', 0, 2, tiled=True)  53.7 us
    all_gather x1, blocking collectives, shards(): gathered = lax.all_gather(params, 'fsdp', axis=0, tiled=False)  18.9 us
    squeeze x1, local copies, waits for them, and re-layouts, chunk_spectrum(): signal[:, index]  8.56 us
    dot_general x1, matrix products, shards(): jnp.dot(group_tokens.reshape(group_rows * block_len, width), in_weight, p...  7.53 us
    dot_general x1, matrix products, chunk_spectrum(): jnp.einsum('fc,sbcd->sbfd', half_lo, blocks, preferred_element_type=jnp.f...  6.29 us
    add x1, other arithmetic, shards(): short_weight[0] * padded[:, :-2] + short_weight[1] * padded[:, 1:-1]  6.29 us
    dot_general x1, matrix products, shards(): jnp.einsum('if,sfd->sid', inverse, spectrum, precision=lax.Precision.HIGH)  5.28 us
  transfers between devices with their start and end apart: 5, of which 2 were waited for; matrix products, arithmetic and copies ran while one was open for 7% of the time, Pallas kernels for 0%

commit v1 on v0

--- a/solution.py
+++ b/solution.py
@@ -84,7 +84,16 @@
     block_counts,
 ):
     seq_dev, block_len, width = tokens.shape
-    group_tokens = lax.all_gather(tokens, "fsdp", axis=0, tiled=True)
+    ways = lax.axis_size("fsdp")
+    up = [(d, (d + 1) % ways) for d in range(ways)]
+    down = [(d, (d - 1) % ways) for d in range(ways)]
+    earlier, later = ([tokens], [tokens])
+    for _ in range(ways // 2):
+        earlier.append(lax.ppermute(earlier[-1], "fsdp", up))
+    for _ in range((ways - 1) // 2):
+        later.append(lax.ppermute(later[-1], "fsdp", down))
+    line = jnp.concatenate([*earlier[::-1], *later[1:]], axis=0)
+    group_tokens = jnp.roll(line, (lax.axis_index("fsdp") - ways // 2) * tokens.shape[0], axis=0)
     group_rows = group_tokens.shape[0]
     local_cols = in_weight.shape[1]
     partial = jnp.dot(

time: 244 us -> 236 us (0.967)
  waiting for transfers between devices: 122 us -> 102 us
  local copies, waits for them, and re-layouts: 37 us -> 44.4 us
  starting transfers between devices: 8.13 us -> 15 us
    all_gather x1 -> x0, waiting for transfers between devices: 67.9 us -> none  [shards(): group_tokens = lax.all_gather(tokens, 'fsdp', axis=0, tiled=True)]
    ppermute x0 -> x3, waiting for transfers between devices: none -> 49.5 us  [the longest x2 38.6 us: shards(): earlier.append(lax.ppermute(earlier[-1], 'fsdp', up))]
    ppermute x0 -> x3, starting transfers between devices: none -> 6.85 us  [the longest x1 3.82 us: shards(): later.append(lax.ppermute(later[-1], 'fsdp', down))]
    unnamed x47 -> x56, local copies, waits for them, and re-layouts: 5.05 us -> 11.1 us
  transfers between devices with their start and end apart: 5 -> 7, of which waited for: 2 -> 4; matrix products, arithmetic and copies ran while one was open for 7% -> 9% of each run, Pallas kernels for 0% -> 0%
where the time goes in v1:
time: 236 us; the launch traced here: 235 us
  waiting for transfers between devices  102 us (43%)
  local copies, waits for them, and re-layouts  44.4 us (19%)
  matrix products  26.2 us (11%)
  blocking collectives  19 us (8%)
  starting transfers between devices  15 us (6%)
  other arithmetic  14.8 us (6%)
  between operations  13.8 us (6%)
    all_to_all x1, waiting for transfers between devices, shards(): projected = lax.all_to_all(partial, 'fsdp', 0, 2, tiled=True)  52.3 us
    ppermute x2, waiting for transfers between devices, shards(): earlier.append(lax.ppermute(earlier[-1], 'fsdp', up))  38.6 us
    all_gather x1, blocking collectives, shards(): gathered = lax.all_gather(params, 'fsdp', axis=0, tiled=False)  19 us
    unnamed x56, local copies, waits for them, and re-layouts  11.1 us
    ppermute x1, waiting for transfers between devices, shards(): later.append(lax.ppermute(later[-1], 'fsdp', down))  10.8 us
    squeeze x1, local copies, waits for them, and re-layouts, chunk_spectrum(): signal[:, index]  8.55 us
    dot_general x1, matrix products, chunk_spectrum(): jnp.einsum('fc,sbcd->sbfd', half_lo, blocks, preferred_element_type=jnp.f...  6.3 us
    add x1, other arithmetic, shards(): short_weight[0] * padded[:, :-2] + short_weight[1] * padded[:, 1:-1]  6.29 us
  transfers between devices with their start and end apart: 7, of which 4 were waited for; matrix products, arithmetic and copies ran while one was open for 9% of the time, Pallas kernels for 0%

profile of v1, /device:TPU:0, one launch (start us, length us, event | category | flops | bytes accessed | tf_op | source)
XLA Modules:
  0.0 235.1 jit_solution(8565896136678591522)
XLA Ops:
  6.5 3.0 %collective-permute-start = (bf16[2,128,1536]{2,1,0:T(8,128)(2,1)}, bf16[2,128,1536]{2,1,0:T(8,128)(2,1)}, u32[]{:S(2)}, u32[]{:S(2)}) collective-permute-start(bf16[2,128,1536]{2,1,0:T(8,128)(2,1)} %param.10), channel_id=1, source_target_pairs={{0,1},{1,2},{2,3},{3,0},{4,5},{5,6},{6,7},{7,4},{8,9},{9,10},{10,1... | collective-permute-start | bytes 2359304 | tf_op jit(solution)/shard_map/ppermute | solution.py:92
  9.6 19.9 %collective-permute-done = bf16[2,128,1536]{2,1,0:T(8,128)(2,1)} collective-permute-done((bf16[2,128,1536]{2,1,0:T(8,128)(2,1)}, bf16[2,128,1536]{2,1,0:T(8,128)(2,1)}, u32[]{:S(2)}, u32[]{:S(2)}) %collective-permute-start) | collective-permute-done | bytes 786464 | tf_op jit(solution)/shard_map/ppermute | solution.py:92
  29.4 3.8 %collective-permute-start.2 = (bf16[2,128,1536]{2,1,0:T(8,128)(2,1)}, bf16[2,128,1536]{2,1,0:T(8,128)(2,1)}, u32[]{:S(2)}, u32[]{:S(2)}) collective-permute-start(bf16[2,128,1536]{2,1,0:T(8,128)(2,1)} %param.10), channel_id=1, source_target_pairs={{0,3},{1,0},{2,1},{3,2},{4,7},{5,4},{6,5},{7,6},{8,11},{9,8},{10,9... | collective-permute-start | bytes 2359304 | tf_op jit(solution)/shard_map/ppermute | solution.py:94
  33.3 18.8 %collective-permute-done.1 = bf16[2,128,1536]{2,1,0:T(8,128)(2,1)} collective-permute-done((bf16[2,128,1536]{2,1,0:T(8,128)(2,1)}, bf16[2,128,1536]{2,1,0:T(8,128)(2,1)}, u32[]{:S(2)}, u32[]{:S(2)}) %collective-permute-start.1) | collective-permute-done | bytes 786464 | tf_op jit(solution)/shard_map/ppermute | solution.py:92
  52.0 1.2 constant_dynamic-update-slice_fusion.7
  53.2 1.2 constant_dynamic-update-slice_fusion.6
  54.4 0.1 constant_dynamic-update-slice_fusion.5
  54.5 10.8 %collective-permute-done.2 = bf16[2,128,1536]{2,1,0:T(8,128)(2,1)} collective-permute-done((bf16[2,128,1536]{2,1,0:T(8,128)(2,1)}, bf16[2,128,1536]{2,1,0:T(8,128)(2,1)}, u32[]{:S(2)}, u32[]{:S(2)}) %collective-permute-start.2) | collective-permute-done | bytes 786464 | tf_op jit(solution)/shard_map/ppermute | solution.py:94
  65.3 1.2 constant_dynamic-update-slice_fusion.4
  66.5 1.2 constant_dynamic-update-slice_fusion.3
  67.7 1.2 constant_dynamic-update-slice_fusion.2
  68.9 0.1 constant_dynamic-update-slice_fusion.1
  69.0 1.2 constant_dynamic-update-slice_fusion
  70.2 0.2 constant_dynamic-slice_fusion
  70.4 5.5 %convolution_convert_fusion = bf16[1024,1152]{1,0:T(8,128)(2,1)} fusion(bf16[1024,1536]{1,0:T(8,128)(2,1)S(1)} %bitcast.99, bf16[1536,1152]{1,0:T(8,128)(2,1)S(1)} %copy-done), kind=kOutput, calls=%fused_computation.2 | convolution fusion | flops 3625058304 | bytes 9043968 | tf_op jit(solution)/shard_map/dot_general | solution.py:99
  75.9 3.8 %all-to-all-start = ((bf16[8,128,1152]{2,1,0:T(8,128)(2,1)}), bf16[8,128,1152]{2,1,0:T(8,128)(2,1)S(1)}, u32[]{:S(2)}, u32[]{:S(2)}) async-start(bf16[8,128,1152]{2,1,0:T(8,128)(2,1)} %bitcast.100), calls=%async_computation | async-start | bytes 4718592 | tf_op jit(solution)/shard_map/all_to_all | solution.py:105
  79.7 0.0 all-gather.4.cloned.1.call-start
  79.7 0.1 slice_reduce_fusion.2
  79.8 0.1 compare_convert_fusion
  79.9 52.3 %all-to-all-done = bf16[8,128,1152]{2,1,0:T(8,128)(2,1)S(1)} async-done(((bf16[8,128,1152]{2,1,0:T(8,128)(2,1)}), bf16[8,128,1152]{2,1,0:T(8,128)(2,1)S(1)}, u32[]{:S(2)}, u32[]{:S(2)}) %all-to-all-start) | async-done | bytes 2359328 | tf_op jit(solution)/shard_map/all_to_all | solution.py:105
  132.2 1.4 copy-done.4
  133.6 3.0 %copy.19 = bf16[4,2,128,1152]{2,3,0,1:T(8,128)(2,1)S(1)} copy(bf16[4,2,128,1152]{3,2,1,0:T(8,128)(2,1)} %bitcast.96) | data formatting | bytes 4718592 | tf_op jit(solution)/shard_map/all_to_all | solution.py:105
  136.7 2.9 %fusion.85 = (bf16[2,1,4608]{1,2,0:T(8,128)(2,1)}, bf16[2,1,4608]{1,2,0:T(8,128)(2,1)}) fusion(bf16[2,128,4608]{1,2,0:T(8,128)(2,1)S(1)} %bitcast.92), kind=kLoop, calls=%fused_computation.162 | loop fusion | bytes 73728 | tf_op jit(solution)/shard_map/slice | solution.py:12
  139.6 2.1 copy.22
  141.7 1.3 collective-permute-start.4
  143.0 2.1 copy.20
  145.1 3.0 %collective-permute-start.3 = (bf16[2,1,4608]{2,0,1:T(2,128)(2,1)S(1)}, bf16[2,1,4608]{2,0,1:T(2,128)(2,1)S(1)}, u32[]{:S(2)}, u32[]{:S(2)}) collective-permute-start(bf16[2,1,4608]{2,0,1:T(2,128)(2,1)S(1)} %copy.20), channel_id=1, source_target_pairs={{0,4},{4,8},{8,12},{1,5},{5,9},{9,13},{2,6},{6,10},{10,14},{3,7},{... | collective-permute-start | bytes 55304 | tf_op jit(solution)/shard_map/ppermute | solution.py:15
  148.2 2.0 copy.23
  150.2 2.0 copy.21
  152.1 6.3 %multiply_add_fusion = f32[2,128,4608]{1,2,0:T(8,128)S(1)} fusion(bf16[2,128,4608]{1,2,0:T(8,128)(2,1)S(1)} %bitcast.93, bf16[2,1,4608]{1,2,0:T(8,128)(2,1)} %copy.23, bf16[2,1,4608]{1,2,0:T(8,128)(2,1)} %copy.21, f32[4608]{0:T(1024)S(1)} %get-tuple-element.6, f32[4608]{0:T(1024)S(1)} %get-tuple-element.7, f32[4608]{0:T(1024)S(1)} %get-tuple-element.5), kind=kLoop, calls=%fused_computation.1 | loop fusion | flops 16515072 | bytes 7170048 | tf_op jit(solution)/shard_map/add | solution.py:108
  158.4 2.1 copy-done.2
  160.5 1.0 fusion.22
  161.6 0.0 all-gather.4.cloned.1.call-update
  161.6 0.1 convert_bitcast_fusion
  161.7 0.1 fusion.68
  161.8 0.1 fusion.71
  161.9 19.0 %all-gather.1 = f32[4,129,384]{2,1,0:T(8,128)S(1)} all-gather(f32[1,129,384]{2,1,0:T(8,128)S(1)} %maximum_bitcast_fusion), channel_id=2, replica_groups=mesh['groups'=2,'seq'=4,'fsdp'=4] {'fsdp'}, dimensions={0}, use_global_device_ids=true | all-gather | bytes 990720 | tf_op jit(solution)/shard_map/all_gather | solution.py:123
  180.9 0.1 slice.154
  181.0 0.5 copy.24
  181.5 0.3 reshape.231
  182.0 0.6 fusion.65
  182.6 2.5 %fusion.26 = f32[1024,64]{1,0:T(8,128)S(1)} fusion(f32[17,64]{1,0:T(8,128)S(1)} %copy-done.18, f32[64]{0:T(128)S(1)} %copy-done.21, f32[1024,8]{0,1:T(8,128)S(1)} %get-tuple-element.33, f32[1024,8]{0,1:T(8,128)S(1)} %get-tuple-element.32, f32[1024,1]{0,1:T(1,128)S(1)} %bitcast.105), kind=kOutput, calls=%fused_computation.45 | convolution fusion | flops 13469696 | bytes 336384 | tf_op jit(solution)/shard_map/dot_general | solution.py:36
  185.1 1.5 broadcast_multiply_fusion.1
  186.7 0.9 select_multiply_fusion.1
  187.6 0.5 negate_select_fusion.2
  188.2 0.7 convolution_bitcast_fusion
  188.8 2.7 %fusion.86 = f32[4,256,1536]{2,1,0:T(8,128)S(1)} fusion(f32[4,256,128]{2,1,0:T(8,128)S(1)} %convolution_bitcast_fusion, f32[128,1536,1]{1,0,2:T(8,128)S(1)} %reshape.231), kind=kOutput, calls=%fused_computation.163 | convolution fusion | flops 1207959552 | bytes 7602176 | tf_op jit(solution)/shard_map/bgk,kd->bgd/dot_general | solution.py:151
  191.5 2.7 %slice_bitcast_fusion.5 = (f32[128,1536]{1,0:T(8,128)}, f32[128,1536]{1,0:T(8,128)}, f32[128,1536]{1,0:T(8,128)}, f32[128,1536]{1,0:T(8,128)}, f32[128,1536]{1,0...) fusion(f32[4,256,1536]{2,1,0:T(8,128)S(1)} %fusion.86), kind=kLoop, calls=%fused_computation.49 | loop fusion | bytes 12582912 | tf_op jit(solution)/shard_map/mul | solution.py:69
  194.2 3.2 %copy.25 = bf16[2,512,1536]{2,1,0:T(8,128)(2,1)S(1)} copy(bf16[2,512,1536]{1,2,0:T(8,128)(2,1)} %all-gather.4.cloned.1.call-done) | data formatting | bytes 6291456 | tf_op jit(solution)/shard_map/all_gather | solution.py:137
  197.4 1.8 fusion.51
  199.2 6.3 %add_bitcast_fusion = f32[2,4,256,1536]{3,2,1,0:T(8,128)} fusion(f32[2,4,1536,256]{2,3,1,0:T(8,128)S(1)} %fusion.51, bf16[2,4,128,1536]{3,2,1,0:T(8,128)(2,1)S(1)} %bitcast.95, f32[128,256]{1,0:T(8,128)S(1)} %get-tuple-element.41, f32[128,256]{1,0:T(8,128)S(1)} %get-tuple-element.40), kind=kOutput, calls=%fused_computation | convolution fusion | flops 808615936 | bytes 28573696 | tf_op jit(solution)/shard_map/fc,sbcd->sbfd/dot_general | solution.py:155
  205.5 8.6 %slice_bitcast_fusion = (f32[2,256,1536]{2,1,0:T(8,128)S(1)}, f32[2,256,1536]{2,1,0:T(8,128)S(1)}, f32[2,256,1536]{2,1,0:T(8,128)}, f32[2,256,1536]{2,1,0:T(8,128)}) fusion(f32[2,4,256,1536]{3,2,1,0:T(8,128)} %add_bitcast_fusion), kind=kLoop, calls=%fused_computation.3 | loop fusion | bytes 25165824 | tf_op jit(solution)/shard_map/squeeze | solution.py:158
  214.1 3.1 %select_subtract_fusion.3 = (f32[2,128,1536]{2,1,0:T(8,128)S(1)}, f32[2,128,1536]{2,1,0:T(8,128)S(1)}) fusion(f32[2,256,1536]{2,1,0:T(8,128)} %get-tuple-element.10, f32[128,1536]{1,0:T(8,128)} %get-tuple-element.18, f32[128,1536]{1,0:T(8,128)} %get-tuple-element.19, pred[128]{0:T(512)(128)(4,1)S(1)} %iota_compare_fusion), kind=kLoop, calls=%fused_computation.38 | loop fusion | flops 3145728 | bytes 7864448 | tf_op jit(solution)/shard_map/sub | solution.py:69
  217.3 0.1 copy-done.3
  217.4 0.2 copy-done.6
  217.6 0.2 copy-done.7
  217.8 0.2 copy-done.8
  218.0 0.2 copy-done.9
  218.3 0.2 copy-done.10
  218.5 0.2 copy-done.11
  218.7 1.9 select_subtract_fusion
  220.7 0.0 copy-start.1
  220.7 5.3 %fusion.23 = bf16[2,128,1536]{1,2,0:T(8,128)(2,1)} fusion(f32[2,128,4608]{1,2,0:T(8,128)} %copy-done.2, f32[2,128,1536]{2,1,0:T(8,128)S(1)} %get-tuple-element.27, f32[2,128,1536]{2,1,0:T(8,128)S(1)} %get-tuple-element.26, f32[2,128,1536]{2,1,0:T(8,128)S(1)} %get-tuple-element.36, f32[2,128,1536]{2,1,0:T(8,128)S(1)} %get-tuple-element.37, ...), kind=kOutput, calls=%fused_computation.30 | convolution fusion | flops 611483648 | bytes 15865856 | tf_op jit(solution)/shard_map/if,sfd->sid/dot_general | solution.py:177
  226.0 2.3 copy.30
  (56 shorter events, 0.3 us)
Async XLA Ops:
  6.5 63.9 %copy-start = (bf16[1536,1152]{1,0:T(8,128)(2,1)S(1)}, bf16[1536,1152]{1,0:T(8,128)(2,1)}, u32[]{:S(2)}) copy-start(bf16[1536,1152]{1,0:T(8,128)(2,1)} %param.11) | copy-start | bytes 10616836
  6.5 22.9 %collective-permute-start = (bf16[2,128,1536]{2,1,0:T(8,128)(2,1)}, bf16[2,128,1536]{2,1,0:T(8,128)(2,1)}, u32[]{:S(2)}, u32[]{:S(2)}) collective-permute-start(bf16[2,128,1536]{2,1,0:T(8,128)(2,1)} %param.10), channel_id=1, source_target_pairs={{0,1},{1,2},{2,3},{3,0},{4,5},{5,6},{6,7},{7,4},{8,9},{9,10},{10,1... | collective-permute-start | bytes 2359304 | tf_op jit(solution)/shard_map/ppermute | solution.py:92
  29.4 22.6 %collective-permute-start.1 = (bf16[2,128,1536]{2,1,0:T(8,128)(2,1)}, bf16[2,128,1536]{2,1,0:T(8,128)(2,1)}, u32[]{:S(2)}, u32[]{:S(2)}) collective-permute-start(bf16[2,128,1536]{2,1,0:T(8,128)(2,1)} %collective-permute-done), channel_id=1, source_target_pairs={{0,1},{1,2},{2,3},{3,0},{4,5},{5,6},{6,7},{7,4},{8,9},{9,10},{10,1... | collective-permute-start | bytes 2359304 | tf_op jit(solution)/shard_map/ppermute | solution.py:92
  29.4 35.9 %collective-permute-start.2 = (bf16[2,128,1536]{2,1,0:T(8,128)(2,1)}, bf16[2,128,1536]{2,1,0:T(8,128)(2,1)}, u32[]{:S(2)}, u32[]{:S(2)}) collective-permute-start(bf16[2,128,1536]{2,1,0:T(8,128)(2,1)} %param.10), channel_id=1, source_target_pairs={{0,3},{1,0},{2,1},{3,2},{4,7},{5,4},{6,5},{7,6},{8,11},{9,8},{10,9... | collective-permute-start | bytes 2359304 | tf_op jit(solution)/shard_map/ppermute | solution.py:94
  33.3 21.2 %copy-start.12 = (bf16[2,128,1536]{2,1,0:T(8,128)(2,1)S(1)}, bf16[2,128,1536]{2,1,0:T(8,128)(2,1)}, u32[]{:S(2)}) copy-start(bf16[2,128,1536]{2,1,0:T(8,128)(2,1)} %param.10) | copy-start | bytes 2359300
  75.8 3.8 %copy-start.16 = (f32[3,4608]{1,0:T(4,128)S(1)}, f32[3,4608]{1,0:T(4,128)}, u32[]{:S(2)}) copy-start(f32[3,4608]{1,0:T(4,128)} %param.12) | copy-start | bytes 165892
  75.9 4.0 %copy-start.22 = (s32[2,1]{0,1:T(1,128)S(1)}, s32[2,1]{0,1:T(1,128)}, u32[]{:S(2)}) copy-start(s32[2,1]{0,1:T(1,128)} %param.19) | copy-start | bytes 28
  75.9 56.4 %all-to-all-start = ((bf16[8,128,1152]{2,1,0:T(8,128)(2,1)}), bf16[8,128,1152]{2,1,0:T(8,128)(2,1)S(1)}, u32[]{:S(2)}, u32[]{:S(2)}) async-start(bf16[8,128,1152]{2,1,0:T(8,128)(2,1)} %bitcast.100), calls=%async_computation | async-start | bytes 4718592 | tf_op jit(solution)/shard_map/all_to_all | solution.py:105
  79.7 114.6 %all-gather.4.cloned.1.call-start = ((), (), s32[]{:S(2)}) async-start(), calls=%async_computation.1 | async-start | bytes 3932160 | tf_op jit(solution)/shard_map/all_gather | solution.py:137
  132.2 1.4 copy-start.4
  141.7 6.5 %collective-permute-start.4 = (bf16[2,1,4608]{2,0,1:T(2,128)(2,1)S(1)}, bf16[2,1,4608]{2,0,1:T(2,128)(2,1)S(1)}, u32[]{:S(2)}, u32[]{:S(2)}) collective-permute-start(bf16[2,1,4608]{2,0,1:T(2,128)(2,1)S(1)} %copy.22), channel_id=1, source_target_pairs={{4,0},{8,4},{12,8},{5,1},{9,5},{13,9},{6,2},{10,6},{14,10},{7,3},{... | collective-permute-start | bytes 55304 | tf_op jit(solution)/shard_map/ppermute | solution.py:17
  145.1 5.0 %collective-permute-start.3 = (bf16[2,1,4608]{2,0,1:T(2,128)(2,1)S(1)}, bf16[2,1,4608]{2,0,1:T(2,128)(2,1)S(1)}, u32[]{:S(2)}, u32[]{:S(2)}) collective-permute-start(bf16[2,1,4608]{2,0,1:T(2,128)(2,1)S(1)} %copy.20), channel_id=1, source_target_pairs={{0,4},{4,8},{8,12},{1,5},{5,9},{9,13},{2,6},{6,10},{10,14},{3,7},{... | collective-permute-start | bytes 55304 | tf_op jit(solution)/shard_map/ppermute | solution.py:15
  158.4 2.1 copy-start.2
  160.5 1.3 copy-start.19
  160.5 1.3 copy-start.15
  180.9 1.6 copy-start.18
  180.9 1.6 copy-start.21
  180.9 4.1 %copy-start.17 = (f32[64,64]{1,0:T(8,128)S(1)}, f32[64,64]{1,0:T(8,128)}, u32[]{:S(2)}) copy-start(f32[64,64]{1,0:T(8,128)} %param.15) | copy-start | bytes 49156
  180.9 4.1 %copy-start.20 = (f32[64]{0:T(128)S(1)}, f32[64]{0:T(128)}, u32[]{:S(2)}) copy-start(f32[64]{0:T(128)} %param.16) | copy-start | bytes 772
  214.1 3.3 %copy-start.3 = (f32[2,256,1536]{2,1,0:T(8,128)S(1)}, f32[2,256,1536]{2,1,0:T(8,128)}, u32[]{:S(2)}) copy-start(f32[2,256,1536]{2,1,0:T(8,128)} %get-tuple-element.11) | copy-start | bytes 9437188
  214.1 3.5 %copy-start.6 = (f32[128,1536]{1,0:T(8,128)S(1)}, f32[128,1536]{1,0:T(8,128)}, u32[]{:S(2)}) copy-start(f32[128,1536]{1,0:T(8,128)} %get-tuple-element.12) | copy-start | bytes 2359300
  214.1 3.7 %copy-start.7 = (f32[128,1536]{1,0:T(8,128)S(1)}, f32[128,1536]{1,0:T(8,128)}, u32[]{:S(2)}) copy-start(f32[128,1536]{1,0:T(8,128)} %get-tuple-element.13) | copy-start | bytes 2359300
  214.1 4.0 %copy-start.8 = (f32[128,1536]{1,0:T(8,128)S(1)}, f32[128,1536]{1,0:T(8,128)}, u32[]{:S(2)}) copy-start(f32[128,1536]{1,0:T(8,128)} %get-tuple-element.14) | copy-start | bytes 2359300
  214.1 4.2 %copy-start.9 = (f32[128,1536]{1,0:T(8,128)S(1)}, f32[128,1536]{1,0:T(8,128)}, u32[]{:S(2)}) copy-start(f32[128,1536]{1,0:T(8,128)} %get-tuple-element.15) | copy-start | bytes 2359300
  214.1 4.4 %copy-start.10 = (f32[128,1536]{1,0:T(8,128)S(1)}, f32[128,1536]{1,0:T(8,128)}, u32[]{:S(2)}) copy-start(f32[128,1536]{1,0:T(8,128)} %get-tuple-element.16) | copy-start | bytes 2359300
  214.1 4.6 %copy-start.11 = (f32[128,1536]{1,0:T(8,128)S(1)}, f32[128,1536]{1,0:T(8,128)}, u32[]{:S(2)}) copy-start(f32[128,1536]{1,0:T(8,128)} %get-tuple-element.17) | copy-start | bytes 2359300
  218.7 1.9 copy-start.5
  218.7 1.9 copy-start.13
  218.7 1.9 copy-start.14
  220.7 7.6 %copy-start.1 = (bf16[1536,1152]{1,0:T(8,128)(2,1)S(1)}, bf16[1536,1152]{1,0:T(8,128)(2,1)}, u32[]{:S(2)}) copy-start(bf16[1536,1152]{1,0:T(8,128)(2,1)} %param.11) | copy-start | bytes 10616836
Sparse Core Ops, SparseCore 0:
  161.7 28.2 all-gather.3
